TPU v7x, 32 devices: a whole 2x2x4 slice. The times are simulated.
32 devices in a mesh: seq: 4 (over y, core), batch: 8 (over z, x).
Axes of the slice: x: 2, y: 2, z: 4, core: 2. Of those that a mesh axis runs over, the one named last changes fastest.
Arguments:
- inputs: bfloat16 [8, 512, 768], P('batch', 'seq'), may hold values from -6 to 6
- cotangent: bfloat16 [8, 512, 768], P('batch', 'seq'), may hold values from -6 to 6
- weight: bfloat16 [768, 2304], replicated, may hold values from -0.125 to 0.125
Outputs:
- grad_input: bfloat16 [8, 512, 768], P('batch', 'seq')
- grad_weight: float32 [768, 2304], P('seq', 'batch')
All inputs are finite; a program needn't handle non-finite values.
Results may differ from a plain program's by a relative error of at most 0.0026.
Values may be sent and summed in bfloat16 or wider, within the bound.
No kernel may reach another device: no remote copies, remote signals or barrier semaphores. Data moves between devices by JAX's collectives and lax.ppermute only.
A program may use at most 64 MiB of HBM per device.

v0:
```python
import math
import jax
import jax.numpy as jnp
from jax import lax
from jax.experimental.layout import Layout, with_layout_constraint
from jax.sharding import PartitionSpec as P

KW = 3
TAP_SPACING = 64
HEADROOM = 12.0
TAG = 16


def extended_2(x, sides, width):
    for axis, dim in sides:
        peers, length = (lax.axis_size(axis), x.shape[dim])
        up = [(i, (i + 1) % peers) for i in range(peers - 1)]
        down = [(j, i) for i, j in up]
        last = lax.slice_in_dim(x, length - width, length, axis=dim)
        first = lax.slice_in_dim(x, 0, width, axis=dim)
        before = lax.ppermute(last, axis, up)
        after = lax.ppermute(first, axis, down)
        x = jnp.concatenate([before, x, after], axis=dim)
    return x


def gelu_factors(values):
    normal_cdf = 0.5 * (1.0 + jax.scipy.special.erf(values / math.sqrt(2.0)))
    density = jnp.exp(-0.5 * values * values) / math.sqrt(2.0 * math.pi)
    return (values * normal_cdf, normal_cdf + values * density)


def exponent_of(values):
    flat = values.reshape(-1, values.shape[-1])
    biggest = jnp.max(jnp.abs(flat), axis=0, keepdims=True)
    return jnp.floor(jnp.log2(jnp.maximum(biggest, 1e-30)))


def encode(values, exponent):
    flat = values.reshape(-1, values.shape[-1])
    scaled = (flat * jnp.exp2(HEADROOM - exponent)).astype(jnp.float16)
    tag = jnp.broadcast_to(exponent.astype(jnp.float16), (TAG, flat.shape[-1]))
    return with_layout_constraint(jnp.concatenate([scaled, tag], axis=0), Layout((0, 1)))


def decode(packed, shape):
    exponent = packed[-TAG : 1 - TAG].astype(jnp.float32)
    values = packed[:-TAG].astype(jnp.float32) * jnp.exp2(exponent - HEADROOM)
    return values.reshape(shape)


def send(values, perm, exponent):
    arrived = lax.ppermute(encode(values, exponent), "batch", perm)
    return decode(with_layout_constraint(arrived, Layout((0, 1))), values.shape)


def reduce_over_batch(columns):
    count = lax.axis_size("batch")
    outer = count // 2
    me = lax.axis_index("batch")
    x = me % 2
    z = me // 2
    pairs = [(i, i ^ 1) for i in range(count)]
    blocks = columns.reshape(outer, 2, -1, columns.shape[1])
    mine = lax.dynamic_index_in_dim(blocks, x, axis=1, keepdims=False)
    theirs = lax.dynamic_index_in_dim(blocks, 1 - x, axis=1, keepdims=False)
    half = outer // 2
    received = jnp.concatenate(
        [
            send(theirs[:half], pairs, exponent_of(theirs[:half])),
            send(theirs[half:], pairs, exponent_of(theirs[half:])),
        ],
        axis=0,
    )
    summed = with_layout_constraint(mine + received, Layout((0, 1, 2)))
    spread = exponent_of(summed)
    total = lax.dynamic_index_in_dim(summed, z, axis=0, keepdims=False)
    for shift in sorted(range(1, outer), key=lambda d: (min(d, outer - d), -d)):
        target = lax.dynamic_index_in_dim(summed, (z + shift) % outer, axis=0, keepdims=False)
        perm = [(2 * q + p, 2 * ((q + shift) % outer) + p) for q in range(outer) for p in range(2)]
        total = total + send(target, perm, spread)
    return with_layout_constraint(total, Layout((0, 1))).T


def gather_over_seq(block, cot, width):
    count = lax.axis_size("seq")
    me = lax.axis_index("seq")
    bits = count.bit_length() - 1
    rows = cot.shape[0]
    last = cot[rows - width :]
    first = cot[:width]
    odd = me % 2 == 1
    stack = block[None]
    for bit in reversed(range(1, bits)):
        pairs = [(i, i ^ 1 << bit) for i in range(count)]
        stack = jnp.concatenate([stack, lax.ppermute(stack, "seq", pairs)], axis=0)
    piece = jnp.where(odd, first, last)
    outgoing = jnp.concatenate([stack.reshape(-1, block.shape[-1]), piece], axis=0)
    incoming = lax.ppermute(outgoing, "seq", [(i, i ^ 1) for i in range(count)])
    near = incoming[-width:]
    stack = jnp.concatenate([stack, incoming[:-width].reshape(stack.shape)], axis=0)
    across = [(i, i + 1) for i in range(1, count - 1, 2)] + [(i, i - 1) for i in range(2, count, 2)]
    far = lax.ppermute(jnp.where(odd, last, first), "seq", across)
    before = jnp.where(odd, near, far)
    after = jnp.where(odd, far, near)
    extended = jnp.concatenate([before, cot, after], axis=0)
    reverse = jnp.array([int(format(v, "0%db" % bits)[::-1], 2) for v in range(count)], jnp.int32)
    order = reverse[jnp.bitwise_xor(me, jnp.arange(count, dtype=jnp.int32))]
    return (jnp.take(stack, order, axis=0).reshape(-1, block.shape[-1]), extended)


def body(inputs, cotangent, weight):
    middle_offset = KW // 2
    reach = middle_offset * TAP_SPACING
    length = inputs.shape[1]
    in_width = inputs.shape[2]
    values = inputs[0].astype(jnp.float32)
    activation, deriv = gelu_factors(values)
    act = activation.astype(jnp.bfloat16)
    seq_count = lax.axis_size("seq")
    batch_count = lax.axis_size("batch")
    counted = batch_count * inputs.shape[0] * length * seq_count
    factor = 1.0 / math.sqrt(float(counted))
    channels = cotangent[0].T.reshape(seq_count, -1, length)
    arrived = lax.all_to_all(channels, "seq", 0, 0, tiled=True)
    own_rows = arrived.shape[1]
    owned = jnp.transpose(arrived, (1, 0, 2)).reshape(own_rows, -1)
    if seq_count >= 2 and seq_count & seq_count - 1 == 0:
        whole_act, extended = gather_over_seq(act, cotangent[0], reach)
    else:
        whole_act = lax.all_gather(act[None], "seq", axis=1, tiled=True)[0]
        extended = extended_2(cotangent, (("seq", 1),), reach)[0]
    count = whole_act.shape[0]
    act_padded = jnp.pad(whole_act, ((reach, reach), (0, 0)))
    updated = []
    for tap_index in range(KW):
        window = lax.slice_in_dim(
            act_padded, tap_index * TAP_SPACING, tap_index * TAP_SPACING + count, axis=0
        )
        updated.append(
            lax.dot_general(
                window, owned, (((0,), (1,)), ((), ())), preferred_element_type=jnp.float32
            )
        )
    local_columns = jnp.concatenate(updated, axis=0) * factor
    local_columns = with_layout_constraint(local_columns, Layout((0, 1)))
    local_columns, extended, deriv = lax.optimization_barrier((local_columns, extended, deriv))
    grad_act = jnp.zeros((length, in_width), jnp.float32)
    for tap_index in range(KW):
        window_start = (2 * middle_offset - tap_index) * TAP_SPACING
        window = lax.slice_in_dim(extended, window_start, window_start + length, axis=0)
        grad_act = grad_act + jnp.dot(
            window,
            weight[:, tap_index * in_width : (tap_index + 1) * in_width],
            preferred_element_type=jnp.float32,
        )
    grad_input = (grad_act * deriv).astype(jnp.bfloat16)[None]
    if batch_count == 8:
        grad_weight = reduce_over_batch(local_columns)
    else:
        pieces = local_columns.reshape(batch_count, -1, own_rows)
        swapped = lax.all_to_all(pieces, "batch", split_axis=0, concat_axis=0, tiled=True)
        grad_weight = jnp.sum(swapped, axis=0).T
    return (grad_input, grad_weight)


def solution(mesh):
    placed = (P("batch", "seq", None), P("batch", "seq", None), P())
    return jax.shard_map(
        body,
        mesh=mesh,
        in_specs=placed,
        out_specs=(P("batch", "seq", None), P("seq", "batch")),
        check_vma=False,
    )
```

profile of v0, /device:TPU:0, one launch (start us, length us, event | category | flops | bytes accessed | tf_op | source)
XLA Modules:
  0.0 54.8 jit_solution(10538124624055871205)
XLA Ops:
  0.6 1.1 %fusion.28 = bf16[1,128,768]{2,1,0:T(8,128)(2,1)S(1)} fusion(bf16[1,128,768]{2,1,0:T(8,128)(2,1)} %param.4), kind=kLoop, calls=%fused_computation.47 | loop fusion | flops 589824 | bytes 393216 | tf_op jit(solution)/shard_map/convert_element_type | solution.py:119
  1.7 3.0 %collective-permute-start = (bf16[1,128,768]{2,1,0:T(8,128)(2,1)S(1)}, bf16[1,128,768]{2,1,0:T(8,128)(2,1)S(1)}, u32[]{:S(2)}, u32[]{:S(2)}) collective-permute-start(bf16[1,128,768]{2,1,0:T(8,128)(2,1)S(1)} %fusion.28), channel_id=1, source_target_pairs={{0,16},{8,24},{16,0},{24,8},{1,17},{9,25},{17,1},{25,9},{2,18},{10... | collective-permute-start | bytes 589832 | tf_op jit(solution)/shard_map/ppermute | solution.py:96
  4.8 1.7 %copy.13 = bf16[768,128]{1,0:T(8,128)(2,1)} copy(bf16[768,128]{0,1:T(8,128)(2,1)} %bitcast.121) | data formatting | bytes 393216 | tf_op jit(solution)/shard_map/transpose | solution.py:124
  6.5 3.4 %all-to-all-start = ((bf16[4,192,128]{2,1,0:T(8,128)(2,1)}), bf16[4,192,128]{2,1,0:T(8,128)(2,1)S(1)}, u32[]{:S(2)}, u32[]{:S(2)}) async-start(bf16[4,192,128]{2,1,0:T(8,128)(2,1)} %bitcast.10), calls=%async_computation | async-start | bytes 393216 | tf_op jit(solution)/shard_map/all_to_all | solution.py:125
  9.9 1.0 %select_bitcast_fusion = (bf16[64,768]{1,0:T(8,128)(2,1)S(1)}, bf16[64,768]{1,0:T(8,128)(2,1)S(1)}) fusion(pred[]{:T(512)S(6)} %eq.9, bf16[1,128,768]{2,1,0:T(8,128)(2,1)} %param.5), kind=kLoop, calls=%fused_computation.76 | loop fusion | flops 98304 | bytes 393217 | tf_op jit(solution)/shard_map/jit(_where)/select_n | solution.py:103
  10.8 0.7 %collective-permute-start.2 = (bf16[64,768]{1,0:T(8,128)(2,1)S(1)}, bf16[64,768]{1,0:T(8,128)(2,1)S(1)}, u32[]{:S(2)}, u32[]{:S(2)}) collective-permute-start(bf16[64,768]{1,0:T(8,128)(2,1)S(1)} %get-tuple-element.25), channel_id=1, source_target_pairs={{8,16},{16,8},{9,17},{17,9},{10,18},{18,10},{11,19},{19,11},{12,20... | collective-permute-start | bytes 294920 | tf_op jit(solution)/shard_map/ppermute | solution.py:103
  11.5 1.3 %gather_fusion = s32[4]{0:T(128)S(1)} fusion(s32[4]{0:T(128)} %constant.123.clone, s32[1024]{0:T(1024)S(1)} %pad_clamp_fusion.1), kind=kCustom, calls=%fused_computation | custom fusion | bytes 48 | tf_op jit(solution)/shard_map/gather | solution.py:108
  12.9 0.0 collective-permute-done
  13.0 3.4 %collective-permute-start.1 = (bf16[320,768]{1,0:T(8,128)(2,1)S(1)}, bf16[320,768]{1,0:T(8,128)(2,1)S(1)}, u32[]{:S(2)}, u32[]{:S(2)}) collective-permute-start(bf16[320,768]{1,0:T(8,128)(2,1)S(1)} %pad_maximum_fusion.1), channel_id=1, source_target_pairs={{0,8},{8,0},{16,24},{24,16},{1,9},{9,1},{17,25},{25,17},{2,10},{10... | collective-permute-start | bytes 1474568 | tf_op jit(solution)/shard_map/ppermute | solution.py:99
  16.4 0.1 broadcast_bitcast_fusion
  16.4 0.0 copy-done.2
  16.4 0.2 fusion.24
  16.6 1.2 %collective-permute-done.1 = bf16[320,768]{1,0:T(8,128)(2,1)S(1)} collective-permute-done((bf16[320,768]{1,0:T(8,128)(2,1)S(1)}, bf16[320,768]{1,0:T(8,128)(2,1)S(1)}, u32[]{:S(2)}, u32[]{:S(2)}) %collective-permute-start.1) | collective-permute-done | bytes 491552 | tf_op jit(solution)/shard_map/ppermute | solution.py:99
  17.9 0.1 pad_maximum_fusion
  18.0 0.6 %gather_fusion.1 = bf16[4,128,768]{2,1,0:T(8,128)(2,1)S(1)} fusion(bf16[4,128,768]{2,1,0:T(8,128)(2,1)S(1)} %pad_maximum_fusion, s32[1024]{0:T(1024)S(1)} %pad_clamp_fusion), kind=kCustom, calls=%fused_computation.1 | custom fusion | bytes 1572880 | tf_op jit(solution)/shard_map/jit(_take)/gather | solution.py:109
  18.6 0.2 bitcast_select_fusion
  18.7 0.0 all-to-all-done
  18.7 0.5 convolution_bitcast_fusion
  19.2 0.4 fusion.12
  19.7 0.4 fusion.11
  20.1 0.0 copy-start
  20.1 0.2 maximum_multiply_fusion
  20.3 0.0 collective-permute-done.2
  20.3 0.7 %copy-done = bf16[1,128,768]{2,1,0:T(8,128)(2,1)S(1)} copy-done((bf16[1,128,768]{2,1,0:T(8,128)(2,1)S(1)}, bf16[1,128,768]{2,1,0:T(8,128)(2,1)}, u32[]{:S(2)}) %copy-start) | copy-done | bytes 196632
  21.0 0.0 copy-start.1
  21.0 0.2 fusion.20
  21.2 0.1 fusion.17
  21.3 0.1 pad_maximum_fusion.5
  21.4 1.6 %collective-permute-start.4 = (f16[592,192]{1,0:T(8,128)(2,1)S(1)}, f16[592,192]{1,0:T(8,128)(2,1)S(1)}, u32[]{:S(2)}, u32[]{:S(2)}) collective-permute-start(f16[592,192]{1,0:T(8,128)(2,1)S(1)} %pad_maximum_fusion.5), channel_id=1, source_target_pairs={{0,1},{1,0},{2,3},{3,2},{4,5},{5,4},{6,7},{7,6},{8,9},{9,8},{10,11... | collective-permute-start | bytes 681992 | tf_op jit(solution)/shard_map/ppermute | solution.py:53
  23.0 0.1 fusion.19
  23.1 0.1 pad_maximum_fusion.4
  23.2 0.6 %collective-permute-start.3 = (f16[592,192]{1,0:T(8,128)(2,1)S(1)}, f16[592,192]{1,0:T(8,128)(2,1)S(1)}, u32[]{:S(2)}, u32[]{:S(2)}) collective-permute-start(f16[592,192]{1,0:T(8,128)(2,1)S(1)} %pad_maximum_fusion.4), channel_id=1, source_target_pairs={{0,1},{1,0},{2,3},{3,2},{4,5},{5,4},{6,7},{7,6},{8,9},{9,8},{10,11... | collective-permute-start | bytes 681992 | tf_op jit(solution)/shard_map/ppermute | solution.py:53
  23.8 0.3 fusion.3
  24.1 0.3 convolution_add_fusion.1
  24.4 7.1 %collective-permute-done.4 = f16[592,192]{1,0:T(8,128)(2,1)S(1)} collective-permute-done((f16[592,192]{1,0:T(8,128)(2,1)S(1)}, f16[592,192]{1,0:T(8,128)(2,1)S(1)}, u32[]{:S(2)}, u32[]{:S(2)}) %collective-permute-start.4) | collective-permute-done | bytes 227360 | tf_op jit(solution)/shard_map/ppermute | solution.py:53
  31.5 5.9 %collective-permute-done.3 = f16[592,192]{1,0:T(8,128)(2,1)S(1)} collective-permute-done((f16[592,192]{1,0:T(8,128)(2,1)S(1)}, f16[592,192]{1,0:T(8,128)(2,1)S(1)}, u32[]{:S(2)}, u32[]{:S(2)}) %collective-permute-start.3) | collective-permute-done | bytes 227360 | tf_op jit(solution)/shard_map/ppermute | solution.py:53
  37.5 0.3 abs_reduce_fusion
  37.8 0.1 fusion.34
  37.9 0.1 pad_maximum_fusion.8
  38.0 2.7 %collective-permute-start.7 = (f16[304,192]{1,0:T(8,128)(2,1)S(1)}, f16[304,192]{1,0:T(8,128)(2,1)S(1)}, u32[]{:S(2)}, u32[]{:S(2)}) collective-permute-start(f16[304,192]{1,0:T(8,128)(2,1)S(1)} %get-tuple-element.29), channel_id=1, source_target_pairs={{0,4},{1,5},{2,6},{3,7},{4,0},{5,1},{6,2},{7,3},{8,12},{9,13},{10,... | collective-permute-start | bytes 350216 | tf_op jit(solution)/shard_map/ppermute | solution.py:53
  40.7 1.0 %fusion.8 = bf16[1,128,768]{2,1,0:T(8,128)(2,1)} fusion(f32[128,768]{1,0:T(8,128)S(1)} %fusion.24, f32[128,768]{1,0:T(8,128)S(1)} %convolution_add_fusion.1, bf16[768,2304]{1,0:T(8,128)(2,1)S(1)} %copy-done.1, bf16[256,768]{1,0:T(8,128)(2,1)S(1)} %pad_maximum_fusion.3), kind=kOutput, calls=%fused_computation.14 | convolution fusion | flops 151289856 | bytes 2359296 | tf_op jit(solution)/shard_map/dot_general | solution.py:152
  41.7 1.6 %collective-permute-start.6 = (f16[304,192]{1,0:T(8,128)(2,1)S(1)}, f16[304,192]{1,0:T(8,128)(2,1)S(1)}, u32[]{:S(2)}, u32[]{:S(2)}) collective-permute-start(f16[304,192]{1,0:T(8,128)(2,1)S(1)} %get-tuple-element.28), channel_id=1, source_target_pairs={{0,2},{1,3},{2,4},{3,5},{4,6},{5,7},{6,0},{7,1},{8,10},{9,11},{10,... | collective-permute-start | bytes 350216 | tf_op jit(solution)/shard_map/ppermute | solution.py:53
  43.3 2.3 %collective-permute-start.5 = (f16[304,192]{1,0:T(8,128)(2,1)S(1)}, f16[304,192]{1,0:T(8,128)(2,1)S(1)}, u32[]{:S(2)}, u32[]{:S(2)}) collective-permute-start(f16[304,192]{1,0:T(8,128)(2,1)S(1)} %get-tuple-element.27), channel_id=1, source_target_pairs={{0,6},{1,7},{2,0},{3,1},{4,2},{5,3},{6,4},{7,5},{8,14},{9,15},{10,... | collective-permute-start | bytes 350216 | tf_op jit(solution)/shard_map/ppermute | solution.py:53
  45.5 6.8 %collective-permute-done.7 = f16[304,192]{1,0:T(8,128)(2,1)S(1)} collective-permute-done((f16[304,192]{1,0:T(8,128)(2,1)S(1)}, f16[304,192]{1,0:T(8,128)(2,1)S(1)}, u32[]{:S(2)}, u32[]{:S(2)}) %collective-permute-start.7) | collective-permute-done | bytes 116768 | tf_op jit(solution)/shard_map/ppermute | solution.py:53
  52.4 0.0 collective-permute-done.6
  52.4 1.4 %collective-permute-done.5 = f16[304,192]{1,0:T(8,128)(2,1)S(1)} collective-permute-done((f16[304,192]{1,0:T(8,128)(2,1)S(1)}, f16[304,192]{1,0:T(8,128)(2,1)S(1)}, u32[]{:S(2)}, u32[]{:S(2)}) %collective-permute-start.5) | collective-permute-done | bytes 116768 | tf_op jit(solution)/shard_map/ppermute | solution.py:53
  53.8 0.1 fusion.37
  53.9 0.9 %copy.20 = f32[192,288]{1,0:T(8,128)} copy(f32[192,288]{0,1:T(8,128)S(1)} %fusion.37) | data formatting | bytes 442368
  (25 shorter events, 0.4 us)
Async XLA Ops:
  0.6 15.8 %copy-start.2 = (bf16[1,128,768]{2,1,0:T(8,128)(2,1)S(1)}, bf16[1,128,768]{2,1,0:T(8,128)(2,1)}, u32[]{:S(2)}) copy-start(bf16[1,128,768]{2,1,0:T(8,128)(2,1)} %param.4) | copy-start | bytes 589828
  1.7 11.1 %collective-permute-start = (bf16[1,128,768]{2,1,0:T(8,128)(2,1)S(1)}, bf16[1,128,768]{2,1,0:T(8,128)(2,1)S(1)}, u32[]{:S(2)}, u32[]{:S(2)}) collective-permute-start(bf16[1,128,768]{2,1,0:T(8,128)(2,1)S(1)} %fusion.28), channel_id=1, source_target_pairs={{0,16},{8,24},{16,0},{24,8},{1,17},{9,25},{17,1},{25,9},{2,18},{10... | collective-permute-start | bytes 589832 | tf_op jit(solution)/shard_map/ppermute | solution.py:96
  6.5 12.2 %all-to-all-start = ((bf16[4,192,128]{2,1,0:T(8,128)(2,1)}), bf16[4,192,128]{2,1,0:T(8,128)(2,1)S(1)}, u32[]{:S(2)}, u32[]{:S(2)}) async-start(bf16[4,192,128]{2,1,0:T(8,128)(2,1)} %bitcast.10), calls=%async_computation | async-start | bytes 393216 | tf_op jit(solution)/shard_map/all_to_all | solution.py:125
  10.8 9.4 %collective-permute-start.2 = (bf16[64,768]{1,0:T(8,128)(2,1)S(1)}, bf16[64,768]{1,0:T(8,128)(2,1)S(1)}, u32[]{:S(2)}, u32[]{:S(2)}) collective-permute-start(bf16[64,768]{1,0:T(8,128)(2,1)S(1)} %get-tuple-element.25), channel_id=1, source_target_pairs={{8,16},{16,8},{9,17},{17,9},{10,18},{18,10},{11,19},{19,11},{12,20... | collective-permute-start | bytes 294920 | tf_op jit(solution)/shard_map/ppermute | solution.py:103
  13.0 4.9 %collective-permute-start.1 = (bf16[320,768]{1,0:T(8,128)(2,1)S(1)}, bf16[320,768]{1,0:T(8,128)(2,1)S(1)}, u32[]{:S(2)}, u32[]{:S(2)}) collective-permute-start(bf16[320,768]{1,0:T(8,128)(2,1)S(1)} %pad_maximum_fusion.1), channel_id=1, source_target_pairs={{0,8},{8,0},{16,24},{24,16},{1,9},{9,1},{17,25},{25,17},{2,10},{10... | collective-permute-start | bytes 1474568 | tf_op jit(solution)/shard_map/ppermute | solution.py:99
  20.1 0.9 %copy-start = (bf16[1,128,768]{2,1,0:T(8,128)(2,1)S(1)}, bf16[1,128,768]{2,1,0:T(8,128)(2,1)}, u32[]{:S(2)}) copy-start(bf16[1,128,768]{2,1,0:T(8,128)(2,1)} %param.5) | copy-start | bytes 589828
  21.0 2.7 %copy-start.1 = (bf16[768,2304]{1,0:T(8,128)(2,1)S(1)}, bf16[768,2304]{1,0:T(8,128)(2,1)}, u32[]{:S(2)}) copy-start(bf16[768,2304]{1,0:T(8,128)(2,1)} %param.6) | copy-start | bytes 10616836
  21.4 10.1 %collective-permute-start.4 = (f16[592,192]{1,0:T(8,128)(2,1)S(1)}, f16[592,192]{1,0:T(8,128)(2,1)S(1)}, u32[]{:S(2)}, u32[]{:S(2)}) collective-permute-start(f16[592,192]{1,0:T(8,128)(2,1)S(1)} %pad_maximum_fusion.5), channel_id=1, source_target_pairs={{0,1},{1,0},{2,3},{3,2},{4,5},{5,4},{6,7},{7,6},{8,9},{9,8},{10,11... | collective-permute-start | bytes 681992 | tf_op jit(solution)/shard_map/ppermute | solution.py:53
  23.2 14.3 %collective-permute-start.3 = (f16[592,192]{1,0:T(8,128)(2,1)S(1)}, f16[592,192]{1,0:T(8,128)(2,1)S(1)}, u32[]{:S(2)}, u32[]{:S(2)}) collective-permute-start(f16[592,192]{1,0:T(8,128)(2,1)S(1)} %pad_maximum_fusion.4), channel_id=1, source_target_pairs={{0,1},{1,0},{2,3},{3,2},{4,5},{5,4},{6,7},{7,6},{8,9},{9,8},{10,11... | collective-permute-start | bytes 681992 | tf_op jit(solution)/shard_map/ppermute | solution.py:53
  38.0 14.3 %collective-permute-start.7 = (f16[304,192]{1,0:T(8,128)(2,1)S(1)}, f16[304,192]{1,0:T(8,128)(2,1)S(1)}, u32[]{:S(2)}, u32[]{:S(2)}) collective-permute-start(f16[304,192]{1,0:T(8,128)(2,1)S(1)} %get-tuple-element.29), channel_id=1, source_target_pairs={{0,4},{1,5},{2,6},{3,7},{4,0},{5,1},{6,2},{7,3},{8,12},{9,13},{10,... | collective-permute-start | bytes 350216 | tf_op jit(solution)/shard_map/ppermute | solution.py:53
  41.7 10.7 %collective-permute-start.6 = (f16[304,192]{1,0:T(8,128)(2,1)S(1)}, f16[304,192]{1,0:T(8,128)(2,1)S(1)}, u32[]{:S(2)}, u32[]{:S(2)}) collective-permute-start(f16[304,192]{1,0:T(8,128)(2,1)S(1)} %get-tuple-element.28), channel_id=1, source_target_pairs={{0,2},{1,3},{2,4},{3,5},{4,6},{5,7},{6,0},{7,1},{8,10},{9,11},{10,... | collective-permute-start | bytes 350216 | tf_op jit(solution)/shard_map/ppermute | solution.py:53
  43.3 10.5 %collective-permute-start.5 = (f16[304,192]{1,0:T(8,128)(2,1)S(1)}, f16[304,192]{1,0:T(8,128)(2,1)S(1)}, u32[]{:S(2)}, u32[]{:S(2)}) collective-permute-start(f16[304,192]{1,0:T(8,128)(2,1)S(1)} %get-tuple-element.27), channel_id=1, source_target_pairs={{0,6},{1,7},{2,0},{3,1},{4,2},{5,3},{6,4},{7,5},{8,14},{9,15},{10,... | collective-permute-start | bytes 350216 | tf_op jit(solution)/shard_map/ppermute | solution.py:53
where the time goes:
time: 55.1 us; the launch traced here: 54.8 us
  waiting for transfers between devices  22.4 us (41%)
  starting transfers between devices  19.1 us (35%)
  local copies, waits for them, and re-layouts  5.33 us (10%)
  other arithmetic  4.04 us (7%)
  matrix products  2.96 us (5%)
  between operations  0.93 us (2%)
    ppermute x5, waiting for transfers between devices, send(): arrived = lax.ppermute(encode(values, exponent), 'batch', perm)  21.1 us
    ppermute x5, starting transfers between devices, send(): arrived = lax.ppermute(encode(values, exponent), 'batch', perm)  8.65 us
    ppermute x1, starting transfers between devices, gather_over_seq(): incoming = lax.ppermute(outgoing, 'seq', [(i, i ^ 1) for i in range(count)])  3.39 us
    all_to_all x1, starting transfers between devices, body(): arrived = lax.all_to_all(channels, 'seq', 0, 0, tiled=True)  3.37 us
    ppermute x1, starting transfers between devices, gather_over_seq(): stack = jnp.concatenate([stack, lax.ppermute(stack, 'seq', pairs)], axis=0)  3.03 us
    transpose x1, local copies, waits for them, and re-layouts, body(): channels = cotangent[0].T.reshape(seq_count, -1, length)  1.74 us
    dot_general x3, matrix products, body(): jnp.dot(window, weight[:, tap_index * in_width:(tap_index + 1) * in_width...  1.66 us
    unnamed x7, local copies, waits for them, and re-layouts  1.57 us
  transfers between devices with their start and end apart: 9, of which 5 were waited for; matrix products, arithmetic and copies ran while one was open for 16% of the time, Pallas kernels for 0%

commit v1 on v0

--- a/solution.py
+++ b/solution.py
@@ -122,7 +122,19 @@
     counted = batch_count * inputs.shape[0] * length * seq_count
     factor = 1.0 / math.sqrt(float(counted))
     channels = cotangent[0].T.reshape(seq_count, -1, length)
-    arrived = lax.all_to_all(channels, "seq", 0, 0, tiled=True)
+    ways, here = (lax.axis_size("seq"), lax.axis_index("seq"))
+    width_2 = channels.shape[0] // ways
+    shape_2 = list(channels.shape)
+    shape_2[0] = width_2
+    height = shape_2[0]
+    shape_2[0] = height * ways
+    full = jnp.zeros(shape_2, channels.dtype)
+    for mask in range(ways):
+        part = lax.dynamic_slice_in_dim(channels, (here ^ mask) * width_2, width_2, axis=0)
+        if mask:
+            part = lax.ppermute(part, "seq", [(d_2, d_2 ^ mask) for d_2 in range(ways)])
+        full = lax.dynamic_update_slice_in_dim(full, part, (here ^ mask) * height, axis=0)
+    arrived = full
     own_rows = arrived.shape[1]
     owned = jnp.transpose(arrived, (1, 0, 2)).reshape(own_rows, -1)
     if seq_count >= 2 and seq_count & seq_count - 1 == 0:

time: 55.1 us -> 63.4 us (1.15)
  local copies, waits for them, and re-layouts: 5.33 us -> 13.3 us
  starting transfers between devices: 19.1 us -> 13.2 us
  waiting for transfers between devices: 22.4 us -> 27.5 us
  other arithmetic: 4.04 us -> 4.95 us
    dynamic_update_slice x0 -> x4, local copies, waits for them, and re-layouts: none -> 8.47 us  [body(): lax.dynamic_update_slice_in_dim(full, part, (here ^ mask) * height, axis=0)]
    ppermute x5, waiting for transfers between devices: 21.1 us -> 24.9 us  [send(): arrived = lax.ppermute(encode(values, exponent), 'batch', perm)]
    all_to_all x1 -> x0, starting transfers between devices: 3.37 us -> none  [body(): arrived = lax.all_to_all(channels, 'seq', 0, 0, tiled=True)]
    ppermute x1, starting transfers between devices: 3.39 us -> 0.07 us  [gather_over_seq(): incoming = lax.ppermute(outgoing, 'seq', [(i, i ^ 1) for i in range(count)])]
    ppermute x0 -> x3, starting transfers between devices: none -> 3.15 us  [body(): part = lax.ppermute(part, 'seq', [(d_2, d_2 ^ mask) for d_2 in range(ways)])]
    ppermute x1, waiting for transfers between devices: 0.01 us -> 2.59 us  [gather_over_seq(): stack = jnp.concatenate([stack, lax.ppermute(stack, 'seq', pairs)], axis=0)]
    ppermute x5, starting transfers between devices: 8.65 us -> 6.82 us  [send(): arrived = lax.ppermute(encode(values, exponent), 'batch', perm)]
    transpose x1 -> x0, local copies, waits for them, and re-layouts: 1.74 us -> none  [body(): channels = cotangent[0].T.reshape(seq_count, -1, length)]
  transfers between devices with their start and end apart: 9 -> 11, of which waited for: 5 -> 6; matrix products, arithmetic and copies ran while one was open for 16% -> 26% of each run, Pallas kernels for 0% -> 0%
where the time goes in v1:
time: 63.4 us; the launch traced here: 63.2 us
  waiting for transfers between devices  27.5 us (43%)
  local copies, waits for them, and re-layouts  13.3 us (21%)
  starting transfers between devices  13.2 us (21%)
  other arithmetic  4.95 us (8%)
  matrix products  3.13 us (5%)
  between operations  1.19 us (2%)
    ppermute x5, waiting for transfers between devices, send(): arrived = lax.ppermute(encode(values, exponent), 'batch', perm)  24.9 us
    dynamic_update_slice x4, local copies, waits for them, and re-layouts, body(): lax.dynamic_update_slice_in_dim(full, part, (here ^ mask) * height, axis=0)  8.47 us
    ppermute x5, starting transfers between devices, send(): arrived = lax.ppermute(encode(values, exponent), 'batch', perm)  6.82 us
    ppermute x3, starting transfers between devices, body(): part = lax.ppermute(part, 'seq', [(d_2, d_2 ^ mask) for d_2 in range(ways)])  3.15 us
    unnamed x11, local copies, waits for them, and re-layouts  2.93 us
    ppermute x1, waiting for transfers between devices, gather_over_seq(): stack = jnp.concatenate([stack, lax.ppermute(stack, 'seq', pairs)], axis=0)  2.59 us
    dot_general x3, matrix products, body(): jnp.dot(window, weight[:, tap_index * in_width:(tap_index + 1) * in_width...  1.83 us
    ppermute x1, starting transfers between devices, gather_over_seq(): stack = jnp.concatenate([stack, lax.ppermute(stack, 'seq', pairs)], axis=0)  1.81 us
  transfers between devices with their start and end apart: 11, of which 6 were waited for; matrix products, arithmetic and copies ran while one was open for 26% of the time, Pallas kernels for 0%

profile of v1, /device:TPU:0, one launch (start us, length us, event | category | flops | bytes accessed | tf_op | source)
XLA Modules:
  0.0 63.2 jit_solution(5078990514911675719)
XLA Ops:
  0.7 1.1 %copy.49 = bf16[1,128,768]{1,2,0:T(8,128)(2,1)S(1)} copy(bf16[1,128,768]{2,1,0:T(8,128)(2,1)} %param.5) | data formatting | bytes 393216 | tf_op args[1]
  1.9 2.5 %collective-permute-start.4 = (bf16[1,192,128]{2,1,0:T(8,128)(2,1)S(1)}, bf16[1,192,128]{2,1,0:T(8,128)(2,1)S(1)}, u32[]{:S(2)}, u32[]{:S(2)}) collective-permute-start(bf16[1,192,128]{2,1,0:T(8,128)(2,1)S(1)} %get-tuple-element.31), channel_id=1, source_target_pairs={{0,24},{8,16},{16,8},{24,0},{1,25},{9,17},{17,9},{25,1},{2,26},{10... | collective-permute-start | bytes 147464 | tf_op jit(solution)/shard_map/ppermute | solution.py:135
  4.3 0.6 %collective-permute-start.3 = (bf16[1,192,128]{2,1,0:T(8,128)(2,1)S(1)}, bf16[1,192,128]{2,1,0:T(8,128)(2,1)S(1)}, u32[]{:S(2)}, u32[]{:S(2)}) collective-permute-start(bf16[1,192,128]{2,1,0:T(8,128)(2,1)S(1)} %get-tuple-element.32), channel_id=1, source_target_pairs={{0,16},{8,24},{16,0},{24,8},{1,17},{9,25},{17,1},{25,9},{2,18},{10... | collective-permute-start | bytes 147464 | tf_op jit(solution)/shard_map/ppermute | solution.py:135
  5.0 1.0 %fusion.28 = bf16[1,128,768]{2,1,0:T(8,128)(2,1)S(1)} fusion(bf16[1,128,768]{2,1,0:T(8,128)(2,1)} %param.4), kind=kLoop, calls=%fused_computation.47 | loop fusion | flops 589824 | bytes 393216 | tf_op jit(solution)/shard_map/convert_element_type | solution.py:119
  6.0 1.8 %collective-permute-start = (bf16[1,128,768]{2,1,0:T(8,128)(2,1)S(1)}, bf16[1,128,768]{2,1,0:T(8,128)(2,1)S(1)}, u32[]{:S(2)}, u32[]{:S(2)}) collective-permute-start(bf16[1,128,768]{2,1,0:T(8,128)(2,1)S(1)} %fusion.28), channel_id=1, source_target_pairs={{0,16},{8,24},{16,0},{24,8},{1,17},{9,25},{17,1},{25,9},{2,18},{10... | collective-permute-start | bytes 589832 | tf_op jit(solution)/shard_map/ppermute | solution.py:96
  7.8 0.8 %select_bitcast_fusion = (bf16[64,768]{0,1:T(8,128)(2,1)}, bf16[64,768]{0,1:T(8,128)(2,1)S(1)}) fusion(pred[]{:T(512)S(6)} %eq.9, bf16[1,128,768]{1,2,0:T(8,128)(2,1)S(1)} %copy.49), kind=kLoop, calls=%fused_computation.74 | loop fusion | flops 98304 | bytes 393217 | tf_op jit(solution)/shard_map/jit(_where)/select_n | solution.py:103
  8.6 1.3 %collective-permute-start.5 = (bf16[64,768]{0,1:T(8,128)(2,1)}, bf16[64,768]{0,1:T(8,128)(2,1)}, u32[]{:S(2)}, u32[]{:S(2)}) collective-permute-start(bf16[64,768]{0,1:T(8,128)(2,1)} %get-tuple-element.29), channel_id=1, source_target_pairs={{8,16},{16,8},{9,17},{17,9},{10,18},{18,10},{11,19},{19,11},{12,20... | collective-permute-start | bytes 294920 | tf_op jit(solution)/shard_map/ppermute | solution.py:103
  10.0 0.6 %gather_fusion = s32[4]{0:T(128)S(1)} fusion(s32[4]{0:T(128)S(1)} %copy-done, s32[1024]{0:T(1024)S(1)} %pad_clamp_fusion.1), kind=kCustom, calls=%fused_computation | custom fusion | bytes 48 | tf_op jit(solution)/shard_map/gather | solution.py:108
  10.6 0.1 copy.51
  10.8 2.6 %collective-permute-done = bf16[1,128,768]{2,1,0:T(8,128)(2,1)S(1)} collective-permute-done((bf16[1,128,768]{2,1,0:T(8,128)(2,1)S(1)}, bf16[1,128,768]{2,1,0:T(8,128)(2,1)S(1)}, u32[]{:S(2)}, u32[]{:S(2)}) %collective-permute-start) | collective-permute-done | bytes 196640 | tf_op jit(solution)/shard_map/ppermute | solution.py:96
  13.6 0.2 fusion.24
  13.9 0.1 copy.53
  14.1 2.1 %dynamic_update_slice.12 = bf16[4,192,128]{2,0,1:T(4,128)(2,1)S(1)} dynamic-update-slice(bf16[4,192,128]{2,0,1:T(4,128)(2,1)S(1)} %broadcast_in_dim.54, bf16[1,192,128]{2,0,1:T(2,128)(2,1)S(1)} %copy.53, s32[]{:T(128)S(6)} %select_n.132, s32[]{:T(128)} %constant.103.clone.1, s32[]{:T(128)} %constant.103.clone.1) | dynamic-update-slice | bytes 98308 | tf_op jit(solution)/shard_map/dynamic_update_slice | solution.py:136
  16.3 2.1 %dynamic_update_slice.13 = bf16[4,192,128]{2,0,1:T(4,128)(2,1)S(1)} dynamic-update-slice(bf16[4,192,128]{2,0,1:T(4,128)(2,1)S(1)} %dynamic_update_slice.12, bf16[1,192,128]{2,0,1:T(2,128)(2,1)S(1)} %copy.54, s32[]{:T(128)S(6)} %select_n.133, s32[]{:T(128)} %constant.103.clone.1, s32[]{:T(128)} %constant.103.clone.1) | dynamic-update-slice | bytes 98308 | tf_op jit(solution)/shard_map/dynamic_update_slice | solution.py:136
  18.4 0.1 copy.55
  18.5 2.1 %dynamic_update_slice.14 = bf16[4,192,128]{2,0,1:T(4,128)(2,1)S(1)} dynamic-update-slice(bf16[4,192,128]{2,0,1:T(4,128)(2,1)S(1)} %dynamic_update_slice.13, bf16[1,192,128]{2,0,1:T(2,128)(2,1)S(1)} %copy.55, s32[]{:T(128)S(6)} %select_n.134, s32[]{:T(128)} %constant.103.clone.1, s32[]{:T(128)} %constant.103.clone.1) | dynamic-update-slice | bytes 98308 | tf_op jit(solution)/shard_map/dynamic_update_slice | solution.py:136
  20.7 2.1 %dynamic_update_slice.15 = bf16[4,192,128]{2,0,1:T(4,128)(2,1)S(1)} dynamic-update-slice(bf16[4,192,128]{2,0,1:T(4,128)(2,1)S(1)} %dynamic_update_slice.14, bf16[1,192,128]{2,0,1:T(2,128)(2,1)S(1)} %copy.56, s32[]{:T(128)S(6)} %select_n.135, s32[]{:T(128)} %constant.103.clone.1, s32[]{:T(128)} %constant.103.clone.1) | dynamic-update-slice | bytes 98308 | tf_op jit(solution)/shard_map/dynamic_update_slice | solution.py:136
  22.9 0.7 %copy-done.3 = bf16[320,768]{1,0:T(8,128)(2,1)} copy-done((bf16[320,768]{1,0:T(8,128)(2,1)}, bf16[320,768]{1,0:T(8,128)(2,1)S(1)}, u32[]{:S(2)}) %copy-start.3) | copy-done | bytes 491544
  23.7 0.1 pad_maximum_fusion
  23.7 0.6 gather_fusion.1
  24.3 0.2 bitcast_select_fusion
  24.5 0.4 fusion.12
  24.9 0.4 fusion.11
  25.3 0.2 copy.69
  25.5 0.5 convolution_bitcast_fusion
  26.0 1.0 %broadcast_select_fusion.1 = (bf16[64,768]{0,1:T(8,128)(2,1)S(1)}, bf16[64,768]{0,1:T(8,128)(2,1)S(1)}) fusion(bf16[64,768]{0,1:T(8,128)(2,1)S(1)} %copy.69, bf16[64,768]{0,1:T(8,128)(2,1)} %collective-permute-done.5, pred[]{:T(512)S(6)} %eq.9), kind=kLoop, calls=%fused_computation.77 | loop fusion | flops 98304 | bytes 393217 | tf_op jit(solution)/shard_map/jit(_where)/select_n | solution.py:104
  27.0 0.3 pad_maximum_fusion.3
  27.2 0.2 maximum_multiply_fusion
  27.5 0.2 fusion.20
  27.7 0.1 pad_maximum_fusion.4
  27.8 1.6 %collective-permute-start.6 = (f16[592,192]{1,0:T(8,128)(2,1)S(1)}, f16[592,192]{1,0:T(8,128)(2,1)S(1)}, u32[]{:S(2)}, u32[]{:S(2)}) collective-permute-start(f16[592,192]{1,0:T(8,128)(2,1)S(1)} %pad_maximum_fusion.4), channel_id=1, source_target_pairs={{0,1},{1,0},{2,3},{3,2},{4,5},{5,4},{6,7},{7,6},{8,9},{9,8},{10,11... | collective-permute-start | bytes 681992 | tf_op jit(solution)/shard_map/ppermute | solution.py:53
  29.5 0.1 pad_maximum_fusion.5
  29.6 0.6 collective-permute-start.7
  30.2 0.4 fusion.3
  30.5 0.4 convolution_add_fusion.1
  31.0 6.9 %collective-permute-done.6 = f16[592,192]{1,0:T(8,128)(2,1)S(1)} collective-permute-done((f16[592,192]{1,0:T(8,128)(2,1)S(1)}, f16[592,192]{1,0:T(8,128)(2,1)S(1)}, u32[]{:S(2)}, u32[]{:S(2)}) %collective-permute-start.6) | collective-permute-done | bytes 227360 | tf_op jit(solution)/shard_map/ppermute | solution.py:53
  37.9 6.0 %collective-permute-done.7 = f16[592,192]{1,0:T(8,128)(2,1)S(1)} collective-permute-done((f16[592,192]{1,0:T(8,128)(2,1)S(1)}, f16[592,192]{1,0:T(8,128)(2,1)S(1)}, u32[]{:S(2)}, u32[]{:S(2)}) %collective-permute-start.7) | collective-permute-done | bytes 227360 | tf_op jit(solution)/shard_map/ppermute | solution.py:53
  44.0 0.2 abs_reduce_fusion
  44.3 0.1 fusion.34
  44.4 0.1 pad_maximum_fusion.8
  44.6 3.6 %collective-permute-start.8 = (f16[304,192]{1,0:T(8,128)(2,1)S(1)}, f16[304,192]{1,0:T(8,128)(2,1)S(1)}, u32[]{:S(2)}, u32[]{:S(2)}) collective-permute-start(f16[304,192]{1,0:T(8,128)(2,1)S(1)} %get-tuple-element.35), channel_id=1, source_target_pairs={{0,6},{1,7},{2,0},{3,1},{4,2},{5,3},{6,4},{7,5},{8,14},{9,15},{10,... | collective-permute-start | bytes 350216 | tf_op jit(solution)/shard_map/ppermute | solution.py:53
  48.2 1.1 %fusion.8 = bf16[1,128,768]{2,1,0:T(8,128)(2,1)} fusion(f32[128,768]{1,0:T(8,128)S(1)} %fusion.24, f32[128,768]{1,0:T(8,128)S(1)} %convolution_add_fusion.1, bf16[768,2304]{1,0:T(8,128)(2,1)S(1)} %copy-done.1, bf16[256,768]{0,1:T(8,128)(2,1)S(1)} %pad_maximum_fusion.3), kind=kOutput, calls=%fused_computation.14 | convolution fusion | flops 151289856 | bytes 2359296 | tf_op jit(solution)/shard_map/dot_general | solution.py:164
  49.3 1.0 %collective-permute-start.10 = (f16[304,192]{1,0:T(8,128)(2,1)S(1)}, f16[304,192]{1,0:T(8,128)(2,1)S(1)}, u32[]{:S(2)}, u32[]{:S(2)}) collective-permute-start(f16[304,192]{1,0:T(8,128)(2,1)S(1)} %get-tuple-element.37), channel_id=1, source_target_pairs={{0,4},{1,5},{2,6},{3,7},{4,0},{5,1},{6,2},{7,3},{8,12},{9,13},{10,... | collective-permute-start | bytes 350216 | tf_op jit(solution)/shard_map/ppermute | solution.py:53
  50.3 2.4 %collective-permute-done.8 = f16[304,192]{1,0:T(8,128)(2,1)S(1)} collective-permute-done((f16[304,192]{1,0:T(8,128)(2,1)S(1)}, f16[304,192]{1,0:T(8,128)(2,1)S(1)}, u32[]{:S(2)}, u32[]{:S(2)}) %collective-permute-start.8) | collective-permute-done | bytes 116768 | tf_op jit(solution)/shard_map/ppermute | solution.py:53
  52.7 5.4 %collective-permute-done.9 = f16[304,192]{1,0:T(8,128)(2,1)S(1)} collective-permute-done((f16[304,192]{1,0:T(8,128)(2,1)S(1)}, f16[304,192]{1,0:T(8,128)(2,1)S(1)}, u32[]{:S(2)}, u32[]{:S(2)}) %collective-permute-start.9) | collective-permute-done | bytes 116768 | tf_op jit(solution)/shard_map/ppermute | solution.py:53
  58.1 4.1 %collective-permute-done.10 = f16[304,192]{1,0:T(8,128)(2,1)S(1)} collective-permute-done((f16[304,192]{1,0:T(8,128)(2,1)S(1)}, f16[304,192]{1,0:T(8,128)(2,1)S(1)}, u32[]{:S(2)}, u32[]{:S(2)}) %collective-permute-start.10) | collective-permute-done | bytes 116768 | tf_op jit(solution)/shard_map/ppermute | solution.py:53
  62.2 0.1 fusion.37
  62.3 0.9 %copy.64 = f32[192,288]{1,0:T(8,128)} copy(f32[192,288]{0,1:T(8,128)S(1)} %fusion.37) | data formatting | bytes 442368
  (45 shorter events, 0.9 us)
Async XLA Ops:
  0.6 9.4 %copy-start = (s32[4]{0:T(128)S(1)}, s32[4]{0:T(128)}, u32[]{:S(2)}) copy-start(s32[4]{0:T(128)} %constant.124.clone) | copy-start | bytes 52
  0.6 13.0 %copy-start.2 = (bf16[1,128,768]{2,1,0:T(8,128)(2,1)S(1)}, bf16[1,128,768]{2,1,0:T(8,128)(2,1)}, u32[]{:S(2)}) copy-start(bf16[1,128,768]{2,1,0:T(8,128)(2,1)} %param.4) | copy-start | bytes 589828
  1.9 18.8 %collective-permute-start.4 = (bf16[1,192,128]{2,1,0:T(8,128)(2,1)S(1)}, bf16[1,192,128]{2,1,0:T(8,128)(2,1)S(1)}, u32[]{:S(2)}, u32[]{:S(2)}) collective-permute-start(bf16[1,192,128]{2,1,0:T(8,128)(2,1)S(1)} %get-tuple-element.31), channel_id=1, source_target_pairs={{0,24},{8,16},{16,8},{24,0},{1,25},{9,17},{17,9},{25,1},{2,26},{10... | collective-permute-start | bytes 147464 | tf_op jit(solution)/shard_map/ppermute | solution.py:135
  4.3 14.1 %collective-permute-start.3 = (bf16[1,192,128]{2,1,0:T(8,128)(2,1)S(1)}, bf16[1,192,128]{2,1,0:T(8,128)(2,1)S(1)}, u32[]{:S(2)}, u32[]{:S(2)}) collective-permute-start(bf16[1,192,128]{2,1,0:T(8,128)(2,1)S(1)} %get-tuple-element.32), channel_id=1, source_target_pairs={{0,16},{8,24},{16,0},{24,8},{1,17},{9,25},{17,1},{25,9},{2,18},{10... | collective-permute-start | bytes 147464 | tf_op jit(solution)/shard_map/ppermute | solution.py:135
  5.0 11.2 %collective-permute-start.2 = (bf16[1,192,128]{2,1,0:T(8,128)(2,1)S(1)}, bf16[1,192,128]{2,1,0:T(8,128)(2,1)S(1)}, u32[]{:S(2)}, u32[]{:S(2)}) collective-permute-start(bf16[1,192,128]{2,1,0:T(8,128)(2,1)S(1)} %get-tuple-element.33), channel_id=1, source_target_pairs={{0,8},{8,0},{16,24},{24,16},{1,9},{9,1},{17,25},{25,17},{2,10},{10... | collective-permute-start | bytes 147464 | tf_op jit(solution)/shard_map/ppermute | solution.py:135
  6.0 7.3 %collective-permute-start = (bf16[1,128,768]{2,1,0:T(8,128)(2,1)S(1)}, bf16[1,128,768]{2,1,0:T(8,128)(2,1)S(1)}, u32[]{:S(2)}, u32[]{:S(2)}) collective-permute-start(bf16[1,128,768]{2,1,0:T(8,128)(2,1)S(1)} %fusion.28), channel_id=1, source_target_pairs={{0,16},{8,24},{16,0},{24,8},{1,17},{9,25},{17,1},{25,9},{2,18},{10... | collective-permute-start | bytes 589832 | tf_op jit(solution)/shard_map/ppermute | solution.py:96
  8.6 17.4 %collective-permute-start.5 = (bf16[64,768]{0,1:T(8,128)(2,1)}, bf16[64,768]{0,1:T(8,128)(2,1)}, u32[]{:S(2)}, u32[]{:S(2)}) collective-permute-start(bf16[64,768]{0,1:T(8,128)(2,1)} %get-tuple-element.29), channel_id=1, source_target_pairs={{8,16},{16,8},{9,17},{17,9},{10,18},{18,10},{11,19},{19,11},{12,20... | collective-permute-start | bytes 294920 | tf_op jit(solution)/shard_map/ppermute | solution.py:103
  13.5 9.4 %collective-permute-start.1 = (bf16[320,768]{1,0:T(8,128)(2,1)S(1)}, bf16[320,768]{1,0:T(8,128)(2,1)S(1)}, u32[]{:S(2)}, u32[]{:S(2)}) collective-permute-start(bf16[320,768]{1,0:T(8,128)(2,1)S(1)} %pad_maximum_fusion.1), channel_id=1, source_target_pairs={{0,8},{8,0},{16,24},{24,16},{1,9},{9,1},{17,25},{25,17},{2,10},{10... | collective-permute-start | bytes 1474568 | tf_op jit(solution)/shard_map/ppermute | solution.py:99
  22.9 0.8 %copy-start.3 = (bf16[320,768]{1,0:T(8,128)(2,1)}, bf16[320,768]{1,0:T(8,128)(2,1)S(1)}, u32[]{:S(2)}) copy-start(bf16[320,768]{1,0:T(8,128)(2,1)S(1)} %collective-permute-done.1) | copy-start | bytes 1474564
  24.3 1.0 %slice-start = ((bf16[320,768]{1,0:T(8,128)(2,1)}), bf16[64,768]{1,0:T(8,128)(2,1)S(1)}, s32[]{:S(2)}) async-start(bf16[320,768]{1,0:T(8,128)(2,1)} %copy-done.3), calls=%async_computation | async-start | bytes 196608 | tf_op jit(solution)/shard_map/slice | solution.py:100
  27.4 2.7 %copy-start.1 = (bf16[768,2304]{1,0:T(8,128)(2,1)S(1)}, bf16[768,2304]{1,0:T(8,128)(2,1)}, u32[]{:S(2)}) copy-start(bf16[768,2304]{1,0:T(8,128)(2,1)} %param.6) | copy-start | bytes 10616836
  27.8 10.0 %collective-permute-start.6 = (f16[592,192]{1,0:T(8,128)(2,1)S(1)}, f16[592,192]{1,0:T(8,128)(2,1)S(1)}, u32[]{:S(2)}, u32[]{:S(2)}) collective-permute-start(f16[592,192]{1,0:T(8,128)(2,1)S(1)} %pad_maximum_fusion.4), channel_id=1, source_target_pairs={{0,1},{1,0},{2,3},{3,2},{4,5},{5,4},{6,7},{7,6},{8,9},{9,8},{10,11... | collective-permute-start | bytes 681992 | tf_op jit(solution)/shard_map/ppermute | solution.py:53
  29.6 14.4 %collective-permute-start.7 = (f16[592,192]{1,0:T(8,128)(2,1)S(1)}, f16[592,192]{1,0:T(8,128)(2,1)S(1)}, u32[]{:S(2)}, u32[]{:S(2)}) collective-permute-start(f16[592,192]{1,0:T(8,128)(2,1)S(1)} %pad_maximum_fusion.5), channel_id=1, source_target_pairs={{0,1},{1,0},{2,3},{3,2},{4,5},{5,4},{6,7},{7,6},{8,9},{9,8},{10,11... | collective-permute-start | bytes 681992 | tf_op jit(solution)/shard_map/ppermute | solution.py:53
  44.6 8.1 %collective-permute-start.8 = (f16[304,192]{1,0:T(8,128)(2,1)S(1)}, f16[304,192]{1,0:T(8,128)(2,1)S(1)}, u32[]{:S(2)}, u32[]{:S(2)}) collective-permute-start(f16[304,192]{1,0:T(8,128)(2,1)S(1)} %get-tuple-element.35), channel_id=1, source_target_pairs={{0,6},{1,7},{2,0},{3,1},{4,2},{5,3},{6,4},{7,5},{8,14},{9,15},{10,... | collective-permute-start | bytes 350216 | tf_op jit(solution)/shard_map/ppermute | solution.py:53
  49.3 8.8 %collective-permute-start.9 = (f16[304,192]{1,0:T(8,128)(2,1)S(1)}, f16[304,192]{1,0:T(8,128)(2,1)S(1)}, u32[]{:S(2)}, u32[]{:S(2)}) collective-permute-start(f16[304,192]{1,0:T(8,128)(2,1)S(1)} %get-tuple-element.36), channel_id=1, source_target_pairs={{0,2},{1,3},{2,4},{3,5},{4,6},{5,7},{6,0},{7,1},{8,10},{9,11},{10,... | collective-permute-start | bytes 350216 | tf_op jit(solution)/shard_map/ppermute | solution.py:53
  49.3 12.9 %collective-permute-start.10 = (f16[304,192]{1,0:T(8,128)(2,1)S(1)}, f16[304,192]{1,0:T(8,128)(2,1)S(1)}, u32[]{:S(2)}, u32[]{:S(2)}) collective-permute-start(f16[304,192]{1,0:T(8,128)(2,1)S(1)} %get-tuple-element.37), channel_id=1, source_target_pairs={{0,4},{1,5},{2,6},{3,7},{4,0},{5,1},{6,2},{7,3},{8,12},{9,13},{10,... | collective-permute-start | bytes 350216 | tf_op jit(solution)/shard_map/ppermute | solution.py:53
